TPU v7x, 128 devices: a whole 4x4x4 slice. The times are simulated.
128 devices in a mesh: dp: 8 (over x, core), fsdp: 16 (over y, z).
Axes of the slice: x: 4, y: 4, z: 4, core: 2. Of those that a mesh axis runs over, the one named last changes fastest.
Arguments:
- tokens: bfloat16 [65536, 8192], P(('dp', 'fsdp')), may hold values from -6 to 6
- frozen_value_matrix: bfloat16 [8192, 1024], P('fsdp'), may hold values from -0.0625 to 0.0625
- adapter_down_maps: bfloat16 [512, 64, 8192], P('dp', None, 'fsdp'), may hold values from -0.0625 to 0.0625
- adapter_up_maps: bfloat16 [512, 64, 1024], P('dp', None, 'fsdp'), may hold values from -0.375 to 0.375
- value_output_gradient: bfloat16 [65536, 1024], P(('dp', 'fsdp')), may hold values from -0.125 to 0.125
- window_composer_position: int32 [8, 64], P('dp'), may hold values from 0 to 3
- needed_composers: int32 [8, 4], replicated, may hold values from 0 to 511, as said below
- composer_storage_index: int32 [512], replicated, may hold values from 0 to 511, as said below
Outputs:
- value: bfloat16 [65536, 1024], P(('dp', 'fsdp'))
- grad_down: float32 [512, 64, 8192], P('dp', None, 'fsdp')
- grad_up: float32 [512, 64, 1024], P('dp', None, 'fsdp')
Inputs may be any that keep to these rules, and one draw needn't show every extreme that they name: Every storage index appears once: the adapters and gradients of composer c lie at index composer_storage_index[c]; composer c is owned by index composer_storage_index[c] // 64 of dp. `needed_composers`: the 4 composers of one row have 4 different owners along dp.
All inputs are finite; a program needn't handle non-finite values.
Results may differ from a plain program's by a relative error of at most 0.004.
Values may be sent and summed in bfloat16 or wider, within the bound.
No kernel may reach another device: no remote copies, remote signals or barrier semaphores. Data moves between devices by JAX's collectives and lax.ppermute only.
A program may use at most 128 MiB of HBM per device.

v0:
```python
import jax
import jax.numpy as jnp
from jax import lax
from jax.sharding import PartitionSpec as P

WIN = 128
ADAPTER_SCALE = 2.0


def body(
    tokens,
    frozen_value_matrix,
    adapter_down_maps,
    adapter_up_maps,
    value_output_gradient,
    window_composer_position,
    needed_composers,
    composer_storage_index,
):
    f32, bf16 = (jnp.float32, jnp.bfloat16)
    dp_count = lax.axis_size("dp")
    fsdp_count = lax.axis_size("fsdp")
    group_index = lax.axis_index("dp")
    member_index = lax.axis_index("fsdp")
    tok_rows, width = tokens.shape
    value_cols = frozen_value_matrix.shape[1]
    rank = adapter_down_maps.shape[1]
    each_owner_rows = adapter_down_maps.shape[0]
    down_cols = adapter_down_maps.shape[2]
    up_cols = adapter_up_maps.shape[2]
    list_len = needed_composers.shape[1]
    windows = tok_rows // WIN
    part_cols = value_cols // dp_count
    w_part = lax.dynamic_slice_in_dim(
        frozen_value_matrix, group_index * part_cols, part_cols, axis=1
    )
    w_part_full = lax.all_gather(w_part, "fsdp", axis=0, tiled=True)
    up_x = [(i, (i + 2) % dp_count) for i in range(dp_count)]
    down_x = [(i, (i - 2) % dp_count) for i in range(dp_count)]
    from_left = lax.ppermute(w_part_full, "dp", up_x)
    from_right = lax.ppermute(w_part_full, "dp", down_x)
    half_part = part_cols // 2
    far_a = lax.ppermute(from_left[:, :half_part], "dp", up_x)
    far_b = lax.ppermute(from_right[:, half_part:], "dp", down_x)
    far = jnp.concatenate([far_a, far_b], axis=1)
    same_parity = [w_part_full, from_left, far, from_right]
    w_own = jnp.concatenate(same_parity, axis=1)
    w_partner = lax.ppermute(w_own, "dp", [(i, i ^ 1) for i in range(dp_count)])
    out_own = jnp.dot(tokens, w_own, preferred_element_type=f32)
    out_partner = jnp.dot(tokens, w_partner, preferred_element_type=f32)
    held = jnp.concatenate([out_own, out_partner], axis=1).reshape(tok_rows, dp_count, part_cols)
    part_ids = jnp.arange(dp_count, dtype=jnp.int32)
    partner_index = group_index ^ 1
    same = part_ids % 2 == group_index % 2
    where_held = jnp.where(
        same,
        (group_index - part_ids) % dp_count // 2,
        dp_count // 2 + (partner_index - part_ids) % dp_count // 2,
    )
    frozen_rows = jnp.take(held, where_held, axis=1).reshape(tok_rows, value_cols)
    list_slot = jnp.take(composer_storage_index, needed_composers, axis=0)
    list_owner = list_slot // each_owner_rows
    list_local = list_slot % each_owner_rows
    owned_here = list_owner == group_index
    locally_owned_slots = jnp.sum(jnp.where(owned_here, list_local, 0), axis=1)
    owned_any = jnp.any(owned_here, axis=1)
    send = jnp.concatenate(
        [
            jnp.take(adapter_down_maps, locally_owned_slots, axis=0),
            jnp.take(adapter_up_maps, locally_owned_slots, axis=0),
        ],
        axis=2,
    )
    send = jnp.where(owned_any[:, None, None], send, jnp.zeros((), send.dtype))
    got = lax.all_to_all(send, "dp", split_axis=0, concat_axis=0, tiled=True)
    my_owner = lax.dynamic_index_in_dim(list_owner, group_index, 0, keepdims=False)
    slab = jnp.take(got, my_owner, axis=0)
    shares = lax.all_gather(slab, "fsdp", axis=0, tiled=False)
    full_down = shares[..., :down_cols].transpose(1, 2, 0, 3).reshape(list_len, rank, width)
    full_up = shares[..., down_cols:].transpose(1, 2, 0, 3).reshape(list_len, rank, value_cols)
    group_picks = window_composer_position[0]
    my_picks = lax.dynamic_slice_in_dim(group_picks, member_index * windows, windows, 0)
    slot_range = jnp.arange(list_len, dtype=jnp.int32)
    token_hot = jnp.broadcast_to(
        my_picks[:, None, None] == slot_range[None, None, :], (windows, WIN, list_len)
    ).reshape(tok_rows, list_len)
    hot_f = token_hot.astype(f32)
    down_flat = full_down.reshape(list_len * rank, width)
    up_flat = full_up.reshape(list_len * rank, value_cols)
    low_all = lax.dot_general(
        tokens, down_flat, (((1,), (1,)), ((), ())), preferred_element_type=f32
    ).reshape(tok_rows, list_len, rank)
    low = jnp.sum(low_all * hot_f[:, :, None], axis=1).astype(bf16)
    hot_h = token_hot.astype(bf16)
    masked_low = (hot_h[:, :, None] * low[:, None, :]).reshape(tok_rows, list_len * rank)
    adapter_change = jnp.dot(masked_low, up_flat, preferred_element_type=f32)
    value = (frozen_rows + ADAPTER_SCALE * adapter_change).astype(bf16)
    back_all = lax.dot_general(
        value_output_gradient, up_flat, (((1,), (1,)), ((), ())), preferred_element_type=f32
    ).reshape(tok_rows, list_len, rank)
    back = (ADAPTER_SCALE * jnp.sum(back_all * hot_f[:, :, None], axis=1)).astype(bf16)
    masked_back = (hot_h[:, :, None] * back[:, None, :]).reshape(tok_rows, list_len * rank)
    scaled_masked_low = masked_low * jnp.asarray(ADAPTER_SCALE, bf16)
    contract = (((0,), (0,)), ((), ()))
    part_down = lax.dot_general(masked_back, tokens, contract, preferred_element_type=f32)
    part_up = lax.dot_general(
        scaled_masked_low, value_output_gradient, contract, preferred_element_type=f32
    )
    rows = list_len * rank
    part_down = part_down.reshape(rows, fsdp_count, down_cols).transpose(1, 0, 2)
    part_up = part_up.reshape(rows, fsdp_count, up_cols).transpose(1, 0, 2)
    sum_down = lax.psum_scatter(part_down, "fsdp", scatter_dimension=0, tiled=True)[0]
    sum_up = lax.psum_scatter(part_up, "fsdp", scatter_dimension=0, tiled=True)[0]
    summed = jnp.concatenate([sum_down, sum_up], axis=1)
    owner_range = jnp.arange(dp_count, dtype=jnp.int32)
    to_owner = my_owner[None, :] == owner_range[:, None]
    pick_index = jnp.sum(jnp.where(to_owner, slot_range[None, :], 0), axis=1)
    owner_has = jnp.any(to_owner, axis=1)
    send_grad = jnp.take(summed.reshape(list_len, rank, down_cols + up_cols), pick_index, axis=0)
    send_grad = jnp.where(owner_has[:, None, None], send_grad, 0.0)
    back_grad = lax.all_to_all(send_grad, "dp", split_axis=0, concat_axis=0, tiled=True)
    land = jnp.where(owned_any, locally_owned_slots, 0)
    arrived = jnp.where(owned_any[:, None, None], back_grad, 0.0)
    grad_down = (
        jnp.zeros((each_owner_rows, rank, down_cols), f32).at[land].add(arrived[:, :, :down_cols])
    )
    grad_up = (
        jnp.zeros((each_owner_rows, rank, up_cols), f32).at[land].add(arrived[:, :, down_cols:])
    )
    return (value, grad_down, grad_up)


def solution(mesh):
    return jax.shard_map(
        body,
        mesh=mesh,
        in_specs=(
            P(("dp", "fsdp"), None),
            P("fsdp", None),
            P("dp", None, "fsdp"),
            P("dp", None, "fsdp"),
            P(("dp", "fsdp"), None),
            P("dp", None),
            P(),
            P(),
        ),
        out_specs=(P(("dp", "fsdp"), None), P("dp", None, "fsdp"), P("dp", None, "fsdp")),
        check_vma=False,
    )
```

profile of v0, /device:TPU:1, one launch (start us, length us, event | category | flops | bytes accessed | tf_op | source)
XLA Modules:
  0.0 349.0 jit_solution(12175471088303171875)
XLA Ops:
  7.2 0.8 copy.32
  8.1 1.4 gather_fusion.1
  10.0 1.8 gather_fusion.3
  11.8 2.8 gather_fusion.2
  14.8 1.1 maximum_select_fusion
  15.9 5.8 %all-to-all-start = ((bf16[8,64,576]{2,1,0:T(8,128)(2,1)}), bf16[8,64,576]{2,1,0:T(8,128)(2,1)S(1)}, u32[]{:S(2)}, u32[]{:S(2)}) async-start(bf16[8,64,576]{2,1,0:T(8,128)(2,1)} %maximum_select_fusion), calls=%async_computation | async-start | bytes 1310720 | tf_op jit(solution)/shard_map/all_to_all | solution.py:75
  21.7 10.9 %all-to-all-done = bf16[8,64,576]{2,1,0:T(8,128)(2,1)S(1)} async-done(((bf16[8,64,576]{2,1,0:T(8,128)(2,1)}), bf16[8,64,576]{2,1,0:T(8,128)(2,1)S(1)}, u32[]{:S(2)}, u32[]{:S(2)}) %all-to-all-start) | async-done | bytes 589856 | tf_op jit(solution)/shard_map/all_to_all | solution.py:75
  33.2 0.8 bitcast_select_fusion
  35.8 55.6 %all-gather.5.cloned.1.call-done = bf16[16,4,64,576]{3,2,1,0:T(8,128)(2,1)} async-done(((bf16[1,4,64,576]{3,2,1,0:T(8,128)(2,1)}), bf16[16,4,64,576]{3,2,1,0:T(8,128)(2,1)}) %all-gather.5.cloned.1.call-update) | async-done | bytes 4718608 | tf_op jit(solution)/shard_map/all_gather | solution.py:78
  91.4 1.3 slice_bitcast_fusion.1
  92.7 1.7 copy.36
  94.4 2.1 reshape_reshape.7
  96.5 2.7 slice_bitcast_fusion
  99.2 2.4 copy.35
  101.6 4.4 %copy.48 = bf16[32,8,16,512]{3,1,2,0:T(8,128)(2,1)S(1)} copy(bf16[32,8,16,512]{3,2,1,0:T(8,128)(2,1)S(1)} %bitcast.105) | data formatting | bytes 8388608
  106.5 2.4 fusion.20
  109.1 1.4 convolution_bitcast_fusion.1
  110.6 12.2 %copy.43 = bf16[8192,512]{1,0:T(8,128)(2,1)} copy(bf16[8192,512]{0,1:T(8,128)(2,1)} %bitcast.107) | data formatting | bytes 16777216 | tf_op jit(solution)/shard_map/dot_general | solution.py:105
  122.8 9.2 %convolution_bitcast_fusion = f32[16,256,512]{2,1,0:T(8,128)} fusion(bf16[512,256,1]{0,1,2:T(8,128)(2,1)S(1)} %bitcast.114, bf16[16,512,512]{2,1,0:T(8,128)(2,1)} %bitcast.104), kind=kOutput, calls=%fused_computation.9 | convolution fusion | flops 2147483648 | bytes 17039360 | tf_op jit(solution)/shard_map/dot_general | solution.py:105
  132.0 8.1 %all-gather.3.cloned.1.call-done = bf16[8192,128]{0,1:T(8,128)(2,1)} async-done(((bf16[512,128]{0,1:T(8,128)(2,1)}), bf16[8192,128]{0,1:T(8,128)(2,1)}) %all-gather.3.cloned.1.call-update) | async-done | bytes 2097168 | tf_op jit(solution)/shard_map/all_gather | solution.py:37
  140.1 1.2 collective-permute-start
  141.3 1.5 collective-permute-start.2
  142.8 44.3 %collective-permute-done = bf16[8192,128]{0,1:T(8,128)(2,1)S(1)} collective-permute-done((bf16[8192,128]{0,1:T(8,128)(2,1)}, bf16[8192,128]{0,1:T(8,128)(2,1)S(1)}, u32[]{:S(2)}, u32[]{:S(2)}) %collective-permute-start) | collective-permute-done | bytes 2097184 | tf_op jit(solution)/shard_map/ppermute | solution.py:40
  187.3 3.1 constant_dynamic-update-slice_fusion.4
  190.5 2.7 collective-permute-start.3
  193.1 1.5 constant_dynamic-update-slice_fusion.3
  194.6 16.0 %collective-permute-done.1 = bf16[8192,64]{0,1:T(8,128)(2,1)S(1)} collective-permute-done((bf16[8192,64]{0,1:T(8,128)(2,1)S(1)}, bf16[8192,64]{0,1:T(8,128)(2,1)S(1)}, u32[]{:S(2)}, u32[]{:S(2)}) %collective-permute-start.1) | collective-permute-done | bytes 1048608 | tf_op jit(solution)/shard_map/ppermute | solution.py:43
  210.6 1.0 constant_dynamic-update-slice_fusion.2
  211.7 1.2 collective-permute-done.3
  212.8 1.0 constant_dynamic-update-slice_fusion.1
  213.9 1.5 constant_dynamic-update-slice_fusion
  215.3 3.7 %collective-permute-start.4 = (bf16[8192,512]{0,1:T(8,128)(2,1)}, bf16[8192,512]{0,1:T(8,128)(2,1)}, u32[]{:S(2)}, u32[]{:S(2)}) collective-permute-start(bf16[8192,512]{0,1:T(8,128)(2,1)} %constant_dynamic-update-slice_fusion), channel_id=1, source_target_pairs={{0,16},{16,0},{32,48},{48,32},{64,80},{80,64},{96,112},{112,96},{1... | collective-permute-start | bytes 25165832 | tf_op jit(solution)/shard_map/ppermute | solution.py:48
  219.3 11.3 %convolution_bitcast_fusion.3 = f32[512,512]{0,1:T(8,128)} fusion(bf16[8192,512]{0,1:T(8,128)(2,1)} %constant_dynamic-update-slice_fusion, bf16[512,8192]{1,0:T(8,128)(2,1)} %param.8), kind=kOutput, calls=%fused_computation.14 | convolution fusion | flops 4294967296 | bytes 17825792 | tf_op jit(solution)/shard_map/dot_general | solution.py:49
  230.6 0.9 copy.45
  231.5 72.0 %reduce-scatter.7.cloned.1.call-done = f32[1,256,512]{2,1,0:T(8,128)} async-done(((f32[16,256,512]{2,1,0:T(8,128)}), f32[1,256,512]{2,1,0:T(8,128)}) %reduce-scatter.7.cloned.1.call-update) | async-done | bytes 524304
  303.5 1.1 pad_maximum_fusion.1
  305.2 1.3 select_select_fusion
  306.5 6.2 %all-to-all-start.1 = ((f32[8,64,576]{2,1,0:T(8,128)}), f32[8,64,576]{2,1,0:T(8,128)}, u32[]{:S(2)}, u32[]{:S(2)}) async-start(f32[8,64,576]{2,1,0:T(8,128)} %select_select_fusion), calls=%async_computation.1 | async-start | bytes 2621440 | tf_op jit(solution)/shard_map/all_to_all | solution.py:121
  312.6 9.6 %convolution_bitcast_fusion.2 = f32[512,512]{0,1:T(8,128)S(1)} fusion(bf16[8192,512]{0,1:T(8,128)(2,1)} %collective-permute-done.4, bf16[512,8192]{1,0:T(8,128)(2,1)} %param.8), kind=kOutput, calls=%fused_computation.13 | convolution fusion | flops 4294967296 | bytes 17825792 | tf_op jit(solution)/shard_map/dot_general | solution.py:50
  322.4 2.0 gather_fusion
  324.4 1.9 copy.42
  326.4 1.4 add_convert_fusion
  327.8 2.8 all-to-all-done.1
  330.7 1.5 broadcast_select_fusion
  332.3 4.5 %broadcast_in_dim.149 = f32[64,64,512]{2,1,0:T(8,128)} broadcast(f32[]{:T(128)} %constant.200.clone.1), dimensions={} | broadcast | bytes 8388612 | tf_op jit(solution)/shard_map/broadcast_in_dim | solution.py:125
  336.8 3.2 scatter_fusion
  340.2 0.9 scatter_fusion.1
  341.2 1.3 copy-done.5
  (75 shorter events, 5.6 us)
Async XLA Ops:
  7.2 26.9 %copy-start = (bf16[512,1024]{1,0:T(8,128)(2,1)S(1)}, bf16[512,1024]{1,0:T(8,128)(2,1)}, u32[]{:S(2)}) copy-start(bf16[512,1024]{1,0:T(8,128)(2,1)} %param.9) | copy-start | bytes 3145732
  9.5 25.5 %copy-start.7 = (s32[1,64]{1,0:T(1,128)S(1)}, s32[1,64]{1,0:T(1,128)}, u32[]{:S(2)}) copy-start(s32[1,64]{1,0:T(1,128)} %param.13) | copy-start | bytes 772
  9.5 25.7 %copy-start.4 = (bf16[512,1024]{1,0:T(8,128)(2,1)S(1)}, bf16[512,1024]{1,0:T(8,128)(2,1)}, u32[]{:S(2)}) copy-start(bf16[512,1024]{1,0:T(8,128)(2,1)} %param.12) | copy-start | bytes 3145732
  15.9 16.7 %all-to-all-start = ((bf16[8,64,576]{2,1,0:T(8,128)(2,1)}), bf16[8,64,576]{2,1,0:T(8,128)(2,1)S(1)}, u32[]{:S(2)}, u32[]{:S(2)}) async-start(bf16[8,64,576]{2,1,0:T(8,128)(2,1)} %maximum_select_fusion), calls=%async_computation | async-start | bytes 1310720 | tf_op jit(solution)/shard_map/all_to_all | solution.py:75
  21.7 69.7 %all-gather.5.cloned.1.call-start = ((), (), s32[]{:S(2)}) async-start(), calls=%async_computation.5 | async-start | bytes 5570560 | tf_op jit(solution)/shard_map/all_gather | solution.py:78
  34.0 106.0 %all-gather.3.cloned.1.call-start = ((), (), s32[]{:S(2)}) async-start(), calls=%async_computation.4 | async-start | bytes 2228224 | tf_op jit(solution)/shard_map/all_gather | solution.py:37
  35.0 195.6 %reduce-scatter.9.cloned.1.call-start = ((), (), s32[]{:S(2)}) async-start(), calls=%async_computation.7 | async-start | bytes 1114112
  96.5 9.5 %copy-start.2 = (bf16[256,1024]{1,0:T(8,128)(2,1)}, bf16[256,1024]{1,0:T(8,128)(2,1)S(1)}, u32[]{:S(2)}) copy-start(bf16[256,1024]{1,0:T(8,128)(2,1)S(1)} %reshape_reshape.7) | copy-start | bytes 1572868
  99.2 7.3 %slice-start = ((s8[8388608]{0:T(1024)(128)(4,1)}), s8[4194304]{0:T(1024)(128)(4,1)S(1)}, s32[]{:S(2)}) async-start(s8[8388608]{0:T(1024)(128)(4,1)} %bitcast.108), calls=%async_computation.8 | async-start | bytes 8388608
  101.6 4.9 %slice-start.1 = ((s8[8388608]{0:T(1024)(128)(4,1)}), s8[4194304]{0:T(1024)(128)(4,1)S(1)}, s32[]{:S(2)}) async-start(s8[8388608]{0:T(1024)(128)(4,1)} %bitcast.108), calls=%async_computation.9 | async-start | bytes 8388608
  110.6 192.9 %reduce-scatter.7.cloned.1.call-start = ((), (), s32[]{:S(2)}) async-start(), calls=%async_computation.6 | async-start | bytes 8912896
  140.1 47.0 %collective-permute-start = (bf16[8192,128]{0,1:T(8,128)(2,1)}, bf16[8192,128]{0,1:T(8,128)(2,1)S(1)}, u32[]{:S(2)}, u32[]{:S(2)}) collective-permute-start(bf16[8192,128]{0,1:T(8,128)(2,1)} %all-gather.3.cloned.1.call-done), channel_id=1, source_target_pairs={{0,32},{16,48},{32,64},{48,80},{64,96},{80,112},{96,0},{112,16},{1... | collective-permute-start | bytes 6291464 | tf_op jit(solution)/shard_map/ppermute | solution.py:40
  141.3 49.1 %collective-permute-start.2 = (bf16[8192,128]{0,1:T(8,128)(2,1)}, bf16[8192,128]{0,1:T(8,128)(2,1)S(1)}, u32[]{:S(2)}, u32[]{:S(2)}) collective-permute-start(bf16[8192,128]{0,1:T(8,128)(2,1)} %all-gather.3.cloned.1.call-done), channel_id=1, source_target_pairs={{0,96},{16,112},{32,0},{48,16},{64,32},{80,48},{96,64},{112,80},{1... | collective-permute-start | bytes 6291464 | tf_op jit(solution)/shard_map/ppermute | solution.py:41
  187.2 23.5 %collective-permute-start.1 = (bf16[8192,64]{0,1:T(8,128)(2,1)S(1)}, bf16[8192,64]{0,1:T(8,128)(2,1)S(1)}, u32[]{:S(2)}, u32[]{:S(2)}) collective-permute-start(bf16[8192,64]{0,1:T(8,128)(2,1)S(1)} %slice.36), channel_id=1, source_target_pairs={{0,32},{16,48},{32,64},{48,80},{64,96},{80,112},{96,0},{112,16},{1... | collective-permute-start | bytes 3145736 | tf_op jit(solution)/shard_map/ppermute | solution.py:43
  190.5 22.4 %collective-permute-start.3 = (bf16[8192,64]{0,1:T(8,128)(2,1)S(1)}, bf16[8192,64]{0,1:T(8,128)(2,1)S(1)}, u32[]{:S(2)}, u32[]{:S(2)}) collective-permute-start(bf16[8192,64]{0,1:T(8,128)(2,1)S(1)} %slice.37), channel_id=1, source_target_pairs={{0,96},{16,112},{32,0},{48,16},{64,32},{80,48},{96,64},{112,80},{1... | collective-permute-start | bytes 3145736 | tf_op jit(solution)/shard_map/ppermute | solution.py:44
  215.3 97.3 %collective-permute-start.4 = (bf16[8192,512]{0,1:T(8,128)(2,1)}, bf16[8192,512]{0,1:T(8,128)(2,1)}, u32[]{:S(2)}, u32[]{:S(2)}) collective-permute-start(bf16[8192,512]{0,1:T(8,128)(2,1)} %constant_dynamic-update-slice_fusion), channel_id=1, source_target_pairs={{0,16},{16,0},{32,48},{48,32},{64,80},{80,64},{96,112},{112,96},{1... | collective-permute-start | bytes 25165832 | tf_op jit(solution)/shard_map/ppermute | solution.py:48
  306.5 24.2 %all-to-all-start.1 = ((f32[8,64,576]{2,1,0:T(8,128)}), f32[8,64,576]{2,1,0:T(8,128)}, u32[]{:S(2)}, u32[]{:S(2)}) async-start(f32[8,64,576]{2,1,0:T(8,128)} %select_select_fusion), calls=%async_computation.1 | async-start | bytes 2621440 | tf_op jit(solution)/shard_map/all_to_all | solution.py:121
  312.6 9.6 %copy-start.6 = (f32[512,512]{0,1:T(8,128)S(1)}, f32[512,512]{0,1:T(8,128)}, u32[]{:S(2)}) copy-start(f32[512,512]{0,1:T(8,128)} %convolution_bitcast_fusion.3) | copy-start | bytes 3145732
  322.4 3.9 %copy-start.3 = (bf16[256,1024]{1,0:T(8,128)(2,1)S(1)}, bf16[256,1024]{1,0:T(8,128)(2,1)}, u32[]{:S(2)}) copy-start(bf16[256,1024]{1,0:T(8,128)(2,1)} %copy-done.2) | copy-start | bytes 1572868
  332.3 10.2 %copy-start.1 = (bf16[512,1024]{1,0:T(8,128)(2,1)S(1)}, bf16[512,1024]{1,0:T(8,128)(2,1)}, u32[]{:S(2)}) copy-start(bf16[512,1024]{1,0:T(8,128)(2,1)} %param.9) | copy-start | bytes 3145732
  341.1 1.3 copy-start.5
Sparse Core Ops, SparseCore 0:
  34.2 57.1 all-gather.4
  93.5 46.5 all-gather.2
  143.9 71.5 reduce-scatter.8
  219.1 84.3 reduce-scatter.6
where the time goes:
time: 350 us; the launch traced here: 349 us
  waiting for transfers between devices  211 us (60%)
  local copies, waits for them, and re-layouts  55.8 us (16%)
  matrix products  35.7 us (10%)
  starting transfers between devices  21.2 us (6%)
  between operations  14.2 us (4%)
  other arithmetic  11 us (3%)
    unnamed x6, waiting for transfers between devices  72.1 us
    all_gather x1, waiting for transfers between devices, body(): shares = lax.all_gather(slab, 'fsdp', axis=0, tiled=False)  55.6 us
    ppermute x1, waiting for transfers between devices, body(): from_left = lax.ppermute(w_part_full, 'dp', up_x)  44.3 us
    ppermute x1, waiting for transfers between devices, body(): far_a = lax.ppermute(from_left[:, :half_part], 'dp', up_x)  16 us
    unnamed x32, local copies, waits for them, and re-layouts  14.7 us
    dot_general x1, local copies, waits for them, and re-layouts, body(): lax.dot_general(masked_back, tokens, contract, preferred_element_type=f32)  12.2 us
    dot_general x1, matrix products, body(): out_own = jnp.dot(tokens, w_own, preferred_element_type=f32)  11.3 us
    all_to_all x1, waiting for transfers between devices, body(): got = lax.all_to_all(send, 'dp', split_axis=0, concat_axis=0, tiled=True)  10.9 us
  transfers between devices with their start and end apart: 11, of which 8 were waited for; matrix products, arithmetic and copies ran while one was open for 23% of the time, Pallas kernels for 0%

commit v1 on v0

--- a/solution.py
+++ b/solution.py
@@ -34,7 +34,9 @@
     w_part = lax.dynamic_slice_in_dim(
         frozen_value_matrix, group_index * part_cols, part_cols, axis=1
     )
-    w_part_full = lax.all_gather(w_part, "fsdp", axis=0, tiled=True)
+    w_part_full = jnp.concatenate(
+        lax.all_to_all(jnp.stack([w_part] * lax.axis_size("fsdp")), "fsdp", 0, 0), axis=0
+    )
     up_x = [(i, (i + 2) % dp_count) for i in range(dp_count)]
     down_x = [(i, (i - 2) % dp_count) for i in range(dp_count)]
     from_left = lax.ppermute(w_part_full, "dp", up_x)

time: 350 us -> 330 us (0.943)
  waiting for transfers between devices: 211 us -> 132 us
  blocking collectives: 0 us -> 34 us
  local copies, waits for them, and re-layouts: 55.8 us -> 79.5 us
    unnamed x6 -> x5, waiting for transfers between devices: 72.1 us -> 0.07 us
    all_to_all x0 -> x1, blocking collectives: none -> 34 us  [body(): lax.all_to_all(jnp.stack([w_part] * lax.axis_size('fsdp')), 'fsdp', 0, 0)]
    concatenate x1, local copies, waits for them, and re-layouts: 1.46 us -> 14.4 us  [body(): w_own = jnp.concatenate(same_parity, axis=1)]
    all_gather x1 -> x0, waiting for transfers between devices: 8.11 us -> none  [body(): w_part_full = lax.all_gather(w_part, 'fsdp', axis=0, tiled=True)]
    slice x1 -> x2, local copies, waits for them, and re-layouts: 0.07 us -> 6.25 us  [body(): far_b = lax.ppermute(from_right[:, half_part:], 'dp', down_x)]
    unnamed x32 -> x33, local copies, waits for them, and re-layouts: 14.7 us -> 8.6 us
    ppermute x0 -> x2, local copies, waits for them, and re-layouts: none -> 4.5 us  [the longest x1 2.73 us: body(): far_b = lax.ppermute(from_right[:, half_part:], 'dp', down_x)]
  transfers between devices with their start and end apart: 11 -> 10, of which waited for: 8 -> 6; matrix products, arithmetic and copies ran while one was open for 23% -> 26% of each run, Pallas kernels for 0% -> 0%
where the time goes in v1:
time: 330 us; the launch traced here: 328 us
  waiting for transfers between devices  132 us (40%)
  local copies, waits for them, and re-layouts  79.5 us (24%)
  matrix products  37.3 us (11%)
  blocking collectives  34 us (10%)
  starting transfers between devices  20.5 us (6%)
  between operations  14.2 us (4%)
  other arithmetic  11 us (3%)
    all_gather x1, waiting for transfers between devices, body(): shares = lax.all_gather(slab, 'fsdp', axis=0, tiled=False)  56.5 us
    ppermute x1, waiting for transfers between devices, body(): from_left = lax.ppermute(w_part_full, 'dp', up_x)  43.7 us
    all_to_all x1, blocking collectives, body(): lax.all_to_all(jnp.stack([w_part] * lax.axis_size('fsdp')), 'fsdp', 0, 0)  34 us
    ppermute x1, waiting for transfers between devices, body(): far_a = lax.ppermute(from_left[:, :half_part], 'dp', up_x)  14.4 us
    concatenate x1, local copies, waits for them, and re-layouts, body(): w_own = jnp.concatenate(same_parity, axis=1)  14.4 us
    dot_general x1, local copies, waits for them, and re-layouts, body(): lax.dot_general(masked_back, tokens, contract, preferred_element_type=f32)  12.2 us
    dot_general x1, matrix products, body(): out_own = jnp.dot(tokens, w_own, preferred_element_type=f32)  11.6 us
    all_to_all x1, waiting for transfers between devices, body(): got = lax.all_to_all(send, 'dp', split_axis=0, concat_axis=0, tiled=True)  10.9 us
  transfers between devices with their start and end apart: 10, of which 6 were waited for; matrix products, arithmetic and copies ran while one was open for 26% of the time, Pallas kernels for 0%

profile of v1, /device:TPU:1, one launch (start us, length us, event | category | flops | bytes accessed | tf_op | source)
XLA Modules:
  0.0 328.4 jit_solution(9056823805985772544)
XLA Ops:
  9.4 1.8 gather_fusion.3
  11.2 2.8 gather_fusion.2
  14.2 1.1 maximum_select_fusion
  15.2 5.8 %all-to-all-start.1 = ((bf16[8,64,576]{2,1,0:T(8,128)(2,1)}), bf16[8,64,576]{2,1,0:T(8,128)(2,1)S(1)}, u32[]{:S(2)}, u32[]{:S(2)}) async-start(bf16[8,64,576]{2,1,0:T(8,128)(2,1)} %maximum_select_fusion), calls=%async_computation.1 | async-start | bytes 1310720 | tf_op jit(solution)/shard_map/all_to_all | solution.py:77
  21.1 10.9 %all-to-all-done.1 = bf16[8,64,576]{2,1,0:T(8,128)(2,1)S(1)} async-done(((bf16[8,64,576]{2,1,0:T(8,128)(2,1)}), bf16[8,64,576]{2,1,0:T(8,128)(2,1)S(1)}, u32[]{:S(2)}, u32[]{:S(2)}) %all-to-all-start.1) | async-done | bytes 589856 | tf_op jit(solution)/shard_map/all_to_all | solution.py:77
  34.3 56.5 %all-gather.2.cloned.1.call-done = bf16[16,4,64,576]{3,2,1,0:T(8,128)(2,1)} async-done(((bf16[1,4,64,576]{3,2,1,0:T(8,128)(2,1)}), bf16[16,4,64,576]{3,2,1,0:T(8,128)(2,1)}) %all-gather.2.cloned.1.call-update) | async-done | bytes 4718608 | tf_op jit(solution)/shard_map/all_gather | solution.py:80
  90.8 1.3 slice_bitcast_fusion.1
  92.1 1.7 copy.63
  93.7 2.1 reshape_reshape.7
  95.9 1.9 fusion.21
  97.8 2.7 slice_bitcast_fusion
  100.5 2.4 copy.62
  102.9 4.4 %copy.74 = bf16[32,8,16,512]{3,1,2,0:T(8,128)(2,1)S(1)} copy(bf16[32,8,16,512]{3,2,1,0:T(8,128)(2,1)S(1)} %bitcast.107) | data formatting | bytes 8388608
  107.3 2.4 fusion.20
  109.9 1.5 convolution_bitcast_fusion.1
  111.4 12.2 %copy.70 = bf16[8192,512]{1,0:T(8,128)(2,1)} copy(bf16[8192,512]{0,1:T(8,128)(2,1)} %bitcast.113) | data formatting | bytes 16777216 | tf_op jit(solution)/shard_map/dot_general | solution.py:107
  123.6 9.0 %convolution_bitcast_fusion = f32[16,256,512]{2,1,0:T(8,128)} fusion(bf16[512,256,1]{0,1,2:T(8,128)(2,1)S(1)} %bitcast.120, bf16[16,512,512]{2,1,0:T(8,128)(2,1)} %bitcast.106), kind=kOutput, calls=%fused_computation.9 | convolution fusion | flops 2147483648 | bytes 17039360 | tf_op jit(solution)/shard_map/dot_general | solution.py:107
  133.0 34.0 %all_to_all.15 = bf16[16,512,128]{1,2,0:T(8,128)(2,1)} all-to-all(bf16[16,512,128]{1,2,0:T(8,128)(2,1)S(1)} %stack.2), channel_id=1, replica_groups=mesh['dp'=8,'fsdp'=16] {'fsdp'}, dimensions={0} | all-to-all | bytes 4194304 | tf_op jit(solution)/shard_map/all_to_all | solution.py:38
  167.0 3.0 copy.53
  170.0 1.1 collective-permute-start
  171.1 1.7 collective-permute-start.2
  172.8 43.7 %collective-permute-done = bf16[8192,128]{1,0:T(8,128)(2,1)S(1)} collective-permute-done((bf16[8192,128]{1,0:T(8,128)(2,1)S(1)}, bf16[8192,128]{1,0:T(8,128)(2,1)S(1)}, u32[]{:S(2)}, u32[]{:S(2)}) %collective-permute-start) | collective-permute-done | bytes 2097184 | tf_op jit(solution)/shard_map/ppermute | solution.py:42
  216.5 1.3 copy-done.3
  217.9 2.8 copy.54
  220.7 3.5 %slice.37 = bf16[8192,64]{1,0:T(8,128)(2,1)} slice(bf16[8192,128]{1,0:T(8,128)(2,1)} %collective-permute-done.2), slice={[0:8192], [64:128]} | slice | bytes 2097152 | tf_op jit(solution)/shard_map/slice | solution.py:46
  224.2 2.7 copy.55
  226.9 2.7 collective-permute-start.3
  229.6 14.4 %collective-permute-done.1 = bf16[8192,64]{0,1:T(8,128)(2,1)S(1)} collective-permute-done((bf16[8192,64]{0,1:T(8,128)(2,1)}, bf16[8192,64]{0,1:T(8,128)(2,1)S(1)}, u32[]{:S(2)}, u32[]{:S(2)}) %collective-permute-start.1) | collective-permute-done | bytes 1048608 | tf_op jit(solution)/shard_map/ppermute | solution.py:45
  244.0 1.8 copy.56
  245.8 3.5 %collective-permute-done.3 = bf16[8192,64]{0,1:T(8,128)(2,1)} collective-permute-done((bf16[8192,64]{0,1:T(8,128)(2,1)}, bf16[8192,64]{0,1:T(8,128)(2,1)}, u32[]{:S(2)}, u32[]{:S(2)}) %collective-permute-start.3) | collective-permute-done | bytes 1048608 | tf_op jit(solution)/shard_map/ppermute | solution.py:46
  249.3 2.7 copy.57
  252.0 14.4 %concatenate.17 = bf16[8192,512]{1,0:T(8,128)(2,1)} concatenate(bf16[8192,128]{1,0:T(8,128)(2,1)S(1)} %bitcast.111, bf16[8192,128]{1,0:T(8,128)(2,1)} %copy-done.3, bf16[8192,64]{1,0:T(8,128)(2,1)} %copy.56, bf16[8192,64]{1,0:T(8,128)(2,1)} %copy.57, bf16[8192,128]{1,0:T(8,128)(2,1)} %collective-permute-done.2), dimensions={1} | concatenate | bytes 16777216 | tf_op jit(solution)/shard_map/concatenate | solution.py:49
  266.4 4.2 %collective-permute-start.4 = (bf16[8192,512]{1,0:T(8,128)(2,1)}, bf16[8192,512]{1,0:T(8,128)(2,1)}, u32[]{:S(2)}, u32[]{:S(2)}) collective-permute-start(bf16[8192,512]{1,0:T(8,128)(2,1)} %concatenate.17), channel_id=1, source_target_pairs={{0,16},{16,0},{32,48},{48,32},{64,80},{80,64},{96,112},{112,96},{1... | collective-permute-start | bytes 25165832 | tf_op jit(solution)/shard_map/ppermute | solution.py:50
  270.9 11.6 %convolution_bitcast_fusion.3 = f32[512,512]{0,1:T(8,128)} fusion(bf16[8192,512]{1,0:T(8,128)(2,1)} %concatenate.17, bf16[512,8192]{1,0:T(8,128)(2,1)} %param.8), kind=kOutput, calls=%fused_computation.14 | convolution fusion | flops 4294967296 | bytes 17825792 | tf_op jit(solution)/shard_map/dot_general | solution.py:51
  282.4 0.9 copy.72
  283.4 1.1 pad_maximum_fusion.1
  285.1 1.3 select_select_fusion
  286.4 5.0 %all-to-all-start.2 = ((f32[8,64,576]{2,1,0:T(8,128)}), f32[8,64,576]{2,1,0:T(8,128)}, u32[]{:S(2)}, u32[]{:S(2)}) async-start(f32[8,64,576]{2,1,0:T(8,128)} %select_select_fusion), calls=%async_computation.2 | async-start | bytes 2621440 | tf_op jit(solution)/shard_map/all_to_all | solution.py:123
  291.4 9.6 %convolution_bitcast_fusion.2 = f32[512,512]{0,1:T(8,128)S(1)} fusion(bf16[8192,512]{1,0:T(8,128)(2,1)} %collective-permute-done.4, bf16[512,8192]{1,0:T(8,128)(2,1)} %param.8), kind=kOutput, calls=%fused_computation.13 | convolution fusion | flops 4294967296 | bytes 17825792 | tf_op jit(solution)/shard_map/dot_general | solution.py:52
  301.2 2.0 gather_fusion
  303.2 2.0 copy.69
  305.2 1.4 add_convert_fusion
  306.6 2.8 all-to-all-done.2
  309.4 1.5 broadcast_select_fusion
  311.0 4.5 %broadcast_in_dim.149 = f32[64,64,512]{2,1,0:T(8,128)} broadcast(f32[]{:T(128)} %constant.200.clone.1), dimensions={} | broadcast | bytes 8388612 | tf_op jit(solution)/shard_map/broadcast_in_dim | solution.py:127
  315.5 3.2 scatter_fusion
  319.7 0.9 scatter_fusion.1
  320.6 1.3 copy-done.8
  (81 shorter events, 7.5 us)
Async XLA Ops:
  7.2 125.5 %copy-start = (bf16[512,1024]{1,0:T(8,128)(2,1)S(1)}, bf16[512,1024]{1,0:T(8,128)(2,1)}, u32[]{:S(2)}) copy-start(bf16[512,1024]{1,0:T(8,128)(2,1)} %param.9) | copy-start | bytes 3145732
  7.2 1.0 copy-start.2
  14.2 19.3 %copy-start.10 = (s32[1,64]{1,0:T(1,128)S(1)}, s32[1,64]{1,0:T(1,128)}, u32[]{:S(2)}) copy-start(s32[1,64]{1,0:T(1,128)} %param.13) | copy-start | bytes 772
  14.2 19.5 %copy-start.7 = (bf16[512,1024]{1,0:T(8,128)(2,1)S(1)}, bf16[512,1024]{1,0:T(8,128)(2,1)}, u32[]{:S(2)}) copy-start(bf16[512,1024]{1,0:T(8,128)(2,1)} %param.12) | copy-start | bytes 3145732
  15.2 16.7 %all-to-all-start.1 = ((bf16[8,64,576]{2,1,0:T(8,128)(2,1)}), bf16[8,64,576]{2,1,0:T(8,128)(2,1)S(1)}, u32[]{:S(2)}, u32[]{:S(2)}) async-start(bf16[8,64,576]{2,1,0:T(8,128)(2,1)} %maximum_select_fusion), calls=%async_computation.1 | async-start | bytes 1310720 | tf_op jit(solution)/shard_map/all_to_all | solution.py:77
  21.0 69.7 %all-gather.2.cloned.1.call-start = ((), (), s32[]{:S(2)}) async-start(), calls=%async_computation.5 | async-start | bytes 5570560 | tf_op jit(solution)/shard_map/all_gather | solution.py:80
  33.4 249.0 %reduce-scatter.9.cloned.1.call-start = ((), (), s32[]{:S(2)}) async-start(), calls=%async_computation.7 | async-start | bytes 1114112
  95.9 4.6 %copy-start.5 = (bf16[256,1024]{1,0:T(8,128)(2,1)}, bf16[256,1024]{1,0:T(8,128)(2,1)S(1)}, u32[]{:S(2)}) copy-start(bf16[256,1024]{1,0:T(8,128)(2,1)S(1)} %reshape_reshape.7) | copy-start | bytes 1572868
  100.5 6.8 %slice-start = ((s8[8388608]{0:T(1024)(128)(4,1)}), s8[4194304]{0:T(1024)(128)(4,1)S(1)}, s32[]{:S(2)}) async-start(s8[8388608]{0:T(1024)(128)(4,1)} %bitcast.114), calls=%async_computation.8 | async-start | bytes 8388608
  102.9 4.4 %slice-start.1 = ((s8[8388608]{0:T(1024)(128)(4,1)}), s8[4194304]{0:T(1024)(128)(4,1)S(1)}, s32[]{:S(2)}) async-start(s8[8388608]{0:T(1024)(128)(4,1)} %bitcast.114), calls=%async_computation.9 | async-start | bytes 8388608
  111.4 172.0 %reduce-scatter.7.cloned.1.call-start = ((), (), s32[]{:S(2)}) async-start(), calls=%async_computation.6 | async-start | bytes 8912896
  170.0 46.5 %collective-permute-start = (bf16[8192,128]{1,0:T(8,128)(2,1)S(1)}, bf16[8192,128]{1,0:T(8,128)(2,1)S(1)}, u32[]{:S(2)}, u32[]{:S(2)}) collective-permute-start(bf16[8192,128]{1,0:T(8,128)(2,1)S(1)} %bitcast.109), channel_id=1, source_target_pairs={{0,32},{16,48},{32,64},{48,80},{64,96},{80,112},{96,0},{112,16},{1... | collective-permute-start | bytes 6291464 | tf_op jit(solution)/shard_map/ppermute | solution.py:42
  171.1 49.5 %collective-permute-start.2 = (bf16[8192,128]{1,0:T(8,128)(2,1)S(1)}, bf16[8192,128]{1,0:T(8,128)(2,1)}, u32[]{:S(2)}, u32[]{:S(2)}) collective-permute-start(bf16[8192,128]{1,0:T(8,128)(2,1)S(1)} %bitcast.110), channel_id=1, source_target_pairs={{0,96},{16,112},{32,0},{48,16},{64,32},{80,48},{96,64},{112,80},{1... | collective-permute-start | bytes 6291464 | tf_op jit(solution)/shard_map/ppermute | solution.py:43
  216.5 1.3 copy-start.3
  220.7 23.4 %collective-permute-start.1 = (bf16[8192,64]{0,1:T(8,128)(2,1)}, bf16[8192,64]{0,1:T(8,128)(2,1)S(1)}, u32[]{:S(2)}, u32[]{:S(2)}) collective-permute-start(bf16[8192,64]{0,1:T(8,128)(2,1)} %copy.54), channel_id=1, source_target_pairs={{0,32},{16,48},{32,64},{48,80},{64,96},{80,112},{96,0},{112,16},{1... | collective-permute-start | bytes 3145736 | tf_op jit(solution)/shard_map/ppermute | solution.py:45
  226.9 22.4 %collective-permute-start.3 = (bf16[8192,64]{0,1:T(8,128)(2,1)}, bf16[8192,64]{0,1:T(8,128)(2,1)}, u32[]{:S(2)}, u32[]{:S(2)}) collective-permute-start(bf16[8192,64]{0,1:T(8,128)(2,1)} %copy.55), channel_id=1, source_target_pairs={{0,96},{16,112},{32,0},{48,16},{64,32},{80,48},{96,64},{112,80},{1... | collective-permute-start | bytes 3145736 | tf_op jit(solution)/shard_map/ppermute | solution.py:46
  266.4 25.0 %collective-permute-start.4 = (bf16[8192,512]{1,0:T(8,128)(2,1)}, bf16[8192,512]{1,0:T(8,128)(2,1)}, u32[]{:S(2)}, u32[]{:S(2)}) collective-permute-start(bf16[8192,512]{1,0:T(8,128)(2,1)} %concatenate.17), channel_id=1, source_target_pairs={{0,16},{16,0},{32,48},{48,32},{64,80},{80,64},{96,112},{112,96},{1... | collective-permute-start | bytes 25165832 | tf_op jit(solution)/shard_map/ppermute | solution.py:50
  286.4 23.0 %all-to-all-start.2 = ((f32[8,64,576]{2,1,0:T(8,128)}), f32[8,64,576]{2,1,0:T(8,128)}, u32[]{:S(2)}, u32[]{:S(2)}) async-start(f32[8,64,576]{2,1,0:T(8,128)} %select_select_fusion), calls=%async_computation.2 | async-start | bytes 2621440 | tf_op jit(solution)/shard_map/all_to_all | solution.py:123
  291.4 9.6 %copy-start.9 = (f32[512,512]{0,1:T(8,128)S(1)}, f32[512,512]{0,1:T(8,128)}, u32[]{:S(2)}) copy-start(f32[512,512]{0,1:T(8,128)} %convolution_bitcast_fusion.3) | copy-start | bytes 3145732
  303.2 2.0 copy-start.6
  310.9 4.6 %copy-start.4 = (f32[8,64,576]{2,1,0:T(8,128)}, f32[8,64,576]{2,1,0:T(8,128)S(1)}, u32[]{:S(2)}) copy-start(f32[8,64,576]{2,1,0:T(8,128)S(1)} %broadcast_select_fusion) | copy-start | bytes 3538948
  315.5 6.4 %copy-start.1 = (bf16[512,1024]{1,0:T(8,128)(2,1)S(1)}, bf16[512,1024]{1,0:T(8,128)(2,1)}, u32[]{:S(2)}) copy-start(bf16[512,1024]{1,0:T(8,128)(2,1)} %param.9) | copy-start | bytes 3145732
  318.7 0.9 slice-start.2
  320.6 1.3 copy-start.8
Sparse Core Ops, SparseCore 0:
  33.5 57.1 all-gather.1
  111.5 80.4 reduce-scatter.8
  195.8 84.8 reduce-scatter.6
